TPU v7x, 512 devices: a whole 4x4x16 slice. The times are simulated.
512 devices in a mesh: section: 8 (over y, core), expert: 64 (over z, x).
Axes of the slice: x: 4, y: 4, z: 16, core: 2. Of those that a mesh axis runs over, the one named last changes fastest.
Arguments:
- tokens: bfloat16 [8, 8192, 2048], P('section', 'expert'), may hold values from -6 to 6
- grad_out: bfloat16 [8, 8192, 2048], P('section', 'expert'), may hold values from -3 to 3
- expert_ids: int32 [8, 8192, 1], P('section', 'expert'), may hold values from 0 to 15; in each aligned block of 128 rows (0 to 127, 128 to 255, ..., all dimensions but the last counted through in order) at most 16 rows name the same one
- route_weight: bfloat16 [8, 8192, 1], P('section', 'expert'), may hold values from 0.25 to 1
- gate_weight: bfloat16 [8, 64, 2048, 256], P('section', 'expert'), may hold values from -0.125 to 0.125
- up_weight: bfloat16 [8, 64, 2048, 256], P('section', 'expert'), may hold values from -0.125 to 0.125
- down_weight: bfloat16 [8, 64, 256, 2048], P('section', 'expert'), may hold values from -0.1875 to 0.1875
Outputs:
- handed_grad: bfloat16 [8, 8192, 2048], P('section', 'expert')
- gate_grad: bfloat16 [8, 8192, 1], P('section', 'expert')
Inputs may be any that keep to these rules, and one draw needn't show every extreme that they name: `expert_ids`: among the route rows of one device, at most 16 name the same expert, and in every draw some expert is named by exactly 16 rows of some device.
All inputs are finite; a program needn't handle non-finite values.
Results may differ from a plain program's by a relative error of at most 0.0058.
Values may be sent and summed in bfloat16 or wider, within the bound.
No kernel may reach another device: no remote copies, remote signals or barrier semaphores. Data moves between devices by JAX's collectives and lax.ppermute only.
A program may use at most 64 MiB of HBM per device.

v0:
```python
import jax
import jax.numpy as jnp
from jax import lax
from jax.sharding import PartitionSpec as P

SPLIT = 4
TOPK = 1


def from_behind(block, axis, distance):
    devices = range(lax.axis_size(axis))
    route = [((i - distance) % len(devices), i) for i in devices]
    return lax.ppermute(block, axis, route)


def expert_terms(rows_x, rows_g, rows_p, w_gate, w_up, w_down):
    lead = rows_x.shape[:2]
    width = rows_x.shape[2]
    flat_x = rows_x.reshape(-1, width)
    flat_g = rows_g.reshape(-1, width)
    flat_p = rows_p.reshape(-1)
    gate = jnp.dot(flat_x, w_gate, preferred_element_type=jnp.float32)
    upval = jnp.dot(flat_x, w_up, preferred_element_type=jnp.float32)
    sig = jax.nn.sigmoid(gate)
    act = gate * sig
    hidden = act * upval
    zeta = lax.dot_general(
        flat_g, w_down, (((1,), (1,)), ((), ())), preferred_element_type=jnp.float32
    )
    part_p = jnp.sum(hidden * zeta, axis=1).astype(jnp.bfloat16)
    d_hidden = flat_p.astype(jnp.float32)[:, None] * zeta
    d_gate = (d_hidden * upval * sig * (1.0 + gate * (1.0 - sig))).astype(jnp.bfloat16)
    d_up = (d_hidden * act).astype(jnp.bfloat16)
    part_x = lax.dot_general(
        d_gate, w_gate, (((1,), (1,)), ((), ())), preferred_element_type=jnp.float32
    )
    part_x = part_x + lax.dot_general(
        d_up, w_up, (((1,), (1,)), ((), ())), preferred_element_type=jnp.float32
    )
    return (part_x.astype(jnp.bfloat16).reshape(lead + (width,)), part_p.reshape(lead))


def on_device(tokens, grad_out, expert_ids, route_weight, gate_weight, up_weight, down_weight):
    feats = tokens[0]
    grads = grad_out[0]
    route_ids = expert_ids[0].reshape(-1)
    route_w = route_weight[0].reshape(-1)
    w_gate = gate_weight[0, 0]
    w_up = up_weight[0, 0]
    w_down = down_weight[0, 0]
    devices = lax.axis_size("expert")
    groups = devices // SPLIT
    tok_count = feats.shape[0]
    width = feats.shape[1]
    rows = tok_count * TOPK
    capacity = 2 * rows // groups
    onehot = (route_ids[:, None] == jnp.arange(groups, dtype=jnp.int32)[None, :]).astype(jnp.int32)
    before = jnp.cumsum(onehot, axis=0) - onehot
    slot = jnp.sum(before * onehot, axis=1)
    place = route_ids * capacity + slot
    table = (place[None, :] == jnp.arange(groups * capacity, dtype=jnp.int32)[:, None]).astype(
        jnp.bfloat16
    )
    rows_x = jnp.repeat(feats, TOPK, axis=0)
    rows_g = jnp.repeat(grads, TOPK, axis=0)
    send_x = jnp.dot(table, rows_x, preferred_element_type=jnp.float32).astype(jnp.bfloat16)
    send_g = jnp.dot(table, rows_g, preferred_element_type=jnp.float32).astype(jnp.bfloat16)
    send_p = jnp.dot(table, route_w[:, None], preferred_element_type=jnp.float32)[:, 0].astype(
        jnp.bfloat16
    )
    full_x = jnp.broadcast_to(
        send_x.reshape(groups, 1, capacity, width), (groups, SPLIT, capacity, width)
    ).reshape(devices, capacity, width)
    full_g = jnp.broadcast_to(
        send_g.reshape(groups, 1, capacity, width), (groups, SPLIT, capacity, width)
    ).reshape(devices, capacity, width)
    full_p = jnp.broadcast_to(
        send_p.reshape(groups, 1, capacity), (groups, SPLIT, capacity)
    ).reshape(devices, capacity)
    part_x, part_p = expert_terms(
        lax.all_to_all(full_x, "expert", split_axis=0, concat_axis=0, tiled=True),
        lax.all_to_all(full_g, "expert", split_axis=0, concat_axis=0, tiled=True),
        lax.all_to_all(full_p, "expert", split_axis=0, concat_axis=0, tiled=True),
        w_gate,
        w_up,
        w_down,
    )
    back_x, back_p = (
        lax.all_to_all(part_x, "expert", split_axis=0, concat_axis=0, tiled=True),
        lax.all_to_all(part_p, "expert", split_axis=0, concat_axis=0, tiled=True),
    )
    total_x = (
        jnp.sum(back_x.astype(jnp.float32).reshape(groups, SPLIT, capacity, width), axis=1)
        .reshape(groups * capacity, width)
        .astype(jnp.bfloat16)
    )
    total_p = (
        jnp.sum(back_p.astype(jnp.float32).reshape(groups, SPLIT, capacity), axis=1)
        .reshape(groups * capacity)
        .astype(jnp.bfloat16)
    )
    route_x = jnp.take(total_x, place, axis=0).astype(jnp.float32)
    input_grad = jnp.sum(route_x.reshape(tok_count, TOPK, width), axis=1).astype(jnp.bfloat16)
    gate_grad = jnp.take(total_p, place, axis=0).reshape(tok_count, TOPK)
    handed = from_behind(input_grad, "section", -1)
    return (handed[None], gate_grad[None])


def solution(mesh):
    in_specs = (
        P("section", "expert", None),
        P("section", "expert", None),
        P("section", "expert", None),
        P("section", "expert", None),
        P("section", "expert", None, None),
        P("section", "expert", None, None),
        P("section", "expert", None, None),
    )
    out_specs = (P("section", "expert", None), P("section", "expert", None))
    return jax.shard_map(
        on_device, mesh=mesh, in_specs=in_specs, out_specs=out_specs, check_vma=False
    )
```

profile of v0, /device:TPU:1, one launch (start us, length us, event | category | flops | bytes accessed | tf_op | source)
XLA Modules:
  0.0 664.7 jit_solution(15037619260780575846)
XLA Ops:
  0.6 0.0 copy-start
  0.7 0.8 fusion.22
  1.5 0.2 reduce_window_sum.11
  1.7 0.8 select_reduce_fusion
  2.5 0.7 compare_and_fusion
  3.2 1.0 fusion.16
  4.2 0.6 copy.10
  4.8 19.1 %all-to-all-start = ((bf16[64,1,16]{2,1,0:T(2,128)(2,1)}), bf16[64,1,16]{2,1,0:T(2,128)(2,1)S(1)}, u32[]{:S(2)}, u32[]{:S(2)}) async-start(bf16[64,1,16]{2,1,0:T(2,128)(2,1)} %copy.10), calls=%async_computation | async-start | bytes 65536 | tf_op jit(solution)/shard_map/all_to_all | solution.py:83
  23.9 1.5 convolution_convert_fusion
  25.4 11.9 %all-to-all-done = bf16[64,1,16]{2,1,0:T(2,128)(2,1)S(1)} async-done(((bf16[64,1,16]{2,1,0:T(2,128)(2,1)}), bf16[64,1,16]{2,1,0:T(2,128)(2,1)S(1)}, u32[]{:S(2)}, u32[]{:S(2)}) %all-to-all-start) | async-done | bytes 2080 | tf_op jit(solution)/shard_map/all_to_all | solution.py:83
  37.3 2.5 broadcast_in_dim.47
  39.8 0.0 copy-start.3
  39.8 5.8 all-to-all-start.2
  45.6 0.0 copy-done.3
  45.6 0.4 convolution_convert_fusion.1
  46.1 182.1 %all-to-all-done.2 = bf16[64,16,2048]{2,1,0:T(8,128)(2,1)} async-done(((bf16[64,16,2048]{2,1,0:T(8,128)(2,1)}), bf16[64,16,2048]{2,1,0:T(8,128)(2,1)}, u32[]{:S(2)}, u32[]{:S(2)}) %all-to-all-start.2) | async-done | bytes 4194336 | tf_op jit(solution)/shard_map/all_to_all | solution.py:81
  228.1 2.5 broadcast_in_dim.45
  230.6 12.8 %all-to-all-start.1 = ((bf16[64,16,2048]{2,1,0:T(8,128)(2,1)}), bf16[64,16,2048]{2,1,0:T(8,128)(2,1)}, u32[]{:S(2)}, u32[]{:S(2)}) async-start(bf16[64,16,2048]{2,1,0:T(8,128)(2,1)} %bitcast.63), calls=%async_computation.1 | async-start | bytes 8388608 | tf_op jit(solution)/shard_map/all_to_all | solution.py:82
  243.4 0.1 convert_reduce_fusion
  243.5 0.1 reshape.155
  243.6 0.0 copy-done
  243.6 0.0 copy-start.1
  243.6 3.6 fusion.2
  247.2 0.0 copy-done.1
  247.2 3.5 fusion.5
  250.7 176.1 %all-to-all-done.1 = bf16[64,16,2048]{2,1,0:T(8,128)(2,1)} async-done(((bf16[64,16,2048]{2,1,0:T(8,128)(2,1)}), bf16[64,16,2048]{2,1,0:T(8,128)(2,1)}, u32[]{:S(2)}, u32[]{:S(2)}) %all-to-all-start.1) | async-done | bytes 4194336 | tf_op jit(solution)/shard_map/all_to_all | solution.py:82
  426.8 3.9 multiply_reduce_fusion
  430.8 0.0 copy-start.2
  430.8 1.6 fusion
  432.4 0.0 copy-done.2
  432.4 3.5 add_convert_fusion
  435.9 0.0 copy-start.4
  435.9 12.2 %all-to-all-start.3 = ((bf16[64,16,2048]{2,1,0:T(8,128)(2,1)}), bf16[64,16,2048]{2,1,0:T(8,128)(2,1)}, u32[]{:S(2)}, u32[]{:S(2)}) async-start(bf16[64,16,2048]{2,1,0:T(8,128)(2,1)} %bitcast.62), calls=%async_computation.3 | async-start | bytes 8388608 | tf_op jit(solution)/shard_map/all_to_all | solution.py:89
  448.1 0.0 copy-done.4
  448.2 183.4 %all-to-all-done.3 = bf16[64,16,2048]{2,1,0:T(8,128)(2,1)} async-done(((bf16[64,16,2048]{2,1,0:T(8,128)(2,1)}), bf16[64,16,2048]{2,1,0:T(8,128)(2,1)}, u32[]{:S(2)}, u32[]{:S(2)}) %all-to-all-start.3) | async-done | bytes 4194336 | tf_op jit(solution)/shard_map/all_to_all | solution.py:89
  631.5 3.0 bitcast_reduce_fusion
  634.5 0.9 gather_fusion
  635.5 0.1 broadcast_select_fusion
  635.6 7.5 %collective-permute-start = (bf16[128,2048]{1,0:T(8,128)(2,1)S(1)}, bf16[128,2048]{1,0:T(8,128)(2,1)S(1)}, u32[]{:S(2)}, u32[]{:S(2)}) collective-permute-start(bf16[128,2048]{1,0:T(8,128)(2,1)S(1)} %broadcast_select_fusion), channel_id=1, source_target_pairs={{64,0},{128,64},{192,128},{256,192},{320,256},{384,320},{448,384},... | collective-permute-start | bytes 1572872 | tf_op jit(solution)/shard_map/ppermute | solution.py:13
  643.1 0.1 convert_element_type.94
  643.2 18.8 %all_to_all.30 = bf16[64,1,16]{2,1,0:T(2,128)(2,1)S(1)} all-to-all(bf16[64,1,16]{2,1,0:T(2,128)(2,1)S(1)} %convert_element_type.94), channel_id=1, replica_groups=mesh['section'=8,'expert'=64] {'expert'}, dimensions={0} | all-to-all | bytes 4096 | tf_op jit(solution)/shard_map/all_to_all | solution.py:90
  662.1 0.1 convert_element_type.92
  662.2 1.2 gather_fusion.1
  663.4 0.5 and_select_fusion
  663.9 0.0 collective-permute-done
  663.9 0.8 copy.15
  (7 shorter events, 0.1 us)
Async XLA Ops:
  0.6 243.0 %copy-start = (bf16[1,1,2048,256]{3,2,1,0:T(8,128)(2,1)S(1)}, bf16[1,1,2048,256]{3,2,1,0:T(8,128)(2,1)}, u32[]{:S(2)}) copy-start(bf16[1,1,2048,256]{3,2,1,0:T(8,128)(2,1)} %param.11) | copy-start | bytes 3145732
  4.8 32.5 %all-to-all-start = ((bf16[64,1,16]{2,1,0:T(2,128)(2,1)}), bf16[64,1,16]{2,1,0:T(2,128)(2,1)S(1)}, u32[]{:S(2)}, u32[]{:S(2)}) async-start(bf16[64,1,16]{2,1,0:T(2,128)(2,1)} %copy.10), calls=%async_computation | async-start | bytes 65536 | tf_op jit(solution)/shard_map/all_to_all | solution.py:83
  39.8 5.8 copy-start.3
  39.8 188.3 %all-to-all-start.2 = ((bf16[64,16,2048]{2,1,0:T(8,128)(2,1)}), bf16[64,16,2048]{2,1,0:T(8,128)(2,1)}, u32[]{:S(2)}, u32[]{:S(2)}) async-start(bf16[64,16,2048]{2,1,0:T(8,128)(2,1)} %bitcast.64), calls=%async_computation.2 | async-start | bytes 8388608 | tf_op jit(solution)/shard_map/all_to_all | solution.py:81
  230.6 196.2 %all-to-all-start.1 = ((bf16[64,16,2048]{2,1,0:T(8,128)(2,1)}), bf16[64,16,2048]{2,1,0:T(8,128)(2,1)}, u32[]{:S(2)}, u32[]{:S(2)}) async-start(bf16[64,16,2048]{2,1,0:T(8,128)(2,1)} %bitcast.63), calls=%async_computation.1 | async-start | bytes 8388608 | tf_op jit(solution)/shard_map/all_to_all | solution.py:82
  243.6 3.6 copy-start.1
  430.8 1.6 copy-start.2
  435.9 12.2 %copy-start.4 = (s32[1,128,1]{1,2,0:T(1,128)S(1)}, s32[1,128,1]{1,2,0:T(1,128)}, u32[]{:S(2)}) copy-start(s32[1,128,1]{1,2,0:T(1,128)} %param.9) | copy-start | bytes 1540
  435.9 195.6 %all-to-all-start.3 = ((bf16[64,16,2048]{2,1,0:T(8,128)(2,1)}), bf16[64,16,2048]{2,1,0:T(8,128)(2,1)}, u32[]{:S(2)}, u32[]{:S(2)}) async-start(bf16[64,16,2048]{2,1,0:T(8,128)(2,1)} %bitcast.62), calls=%async_computation.3 | async-start | bytes 8388608 | tf_op jit(solution)/shard_map/all_to_all | solution.py:89
  635.6 28.4 %collective-permute-start = (bf16[128,2048]{1,0:T(8,128)(2,1)S(1)}, bf16[128,2048]{1,0:T(8,128)(2,1)S(1)}, u32[]{:S(2)}, u32[]{:S(2)}) collective-permute-start(bf16[128,2048]{1,0:T(8,128)(2,1)S(1)} %broadcast_select_fusion), channel_id=1, source_target_pairs={{64,0},{128,64},{192,128},{256,192},{320,256},{384,320},{448,384},... | collective-permute-start | bytes 1572872 | tf_op jit(solution)/shard_map/ppermute | solution.py:13
where the time goes:
time: 666 us; the launch traced here: 665 us
  waiting for transfers between devices  553 us (83%)
  starting transfers between devices  57.5 us (9%)
  matrix products  19 us (3%)
  blocking collectives  18.8 us (3%)
  local copies, waits for them, and re-layouts  8.9 us (1%)
    all_to_all x1, waiting for transfers between devices, on_device(): lax.all_to_all(part_x, 'expert', split_axis=0, concat_axis=0, tiled=True)  183 us
    all_to_all x1, waiting for transfers between devices, on_device(): lax.all_to_all(full_x, 'expert', split_axis=0, concat_axis=0, tiled=True)  182 us
    all_to_all x1, waiting for transfers between devices, on_device(): lax.all_to_all(full_g, 'expert', split_axis=0, concat_axis=0, tiled=True)  176 us
    all_to_all x1, starting transfers between devices, on_device(): lax.all_to_all(full_p, 'expert', split_axis=0, concat_axis=0, tiled=True)  19.1 us
    all_to_all x1, blocking collectives, on_device(): lax.all_to_all(part_p, 'expert', split_axis=0, concat_axis=0, tiled=True)  18.8 us
  transfers between devices with their start and end apart: 5, of which 4 were waited for; matrix products, arithmetic and copies ran while one was open for 2% of the time, Pallas kernels for 0%

commit v1 on v0

v1 whole, which is shorter than its diff:
```python
import jax
import jax.numpy as jnp
from jax import lax
from jax.sharding import Mesh
from jax.sharding import PartitionSpec as P

SPLIT = 4
TOPK = 1
CAP = 16
PAD = 128


def from_behind(block, axis, distance):
    devices = range(lax.axis_size(axis))
    route = [((i - distance) % len(devices), i) for i in devices]
    return lax.ppermute(block, axis, route)


def shard_terms(rows_x, rows_g, rows_p, w_gate, w_up, w_down):
    gate = jnp.dot(rows_x, w_gate, preferred_element_type=jnp.float32)
    upval = jnp.dot(rows_x, w_up, preferred_element_type=jnp.float32)
    sig = jax.nn.sigmoid(gate)
    act = gate * sig
    hidden = act * upval
    zeta = lax.dot_general(
        rows_g, w_down, (((1,), (1,)), ((), ())), preferred_element_type=jnp.float32
    )
    part_p = jnp.sum(hidden * zeta, axis=1).astype(jnp.bfloat16)
    d_hidden = rows_p.astype(jnp.float32)[:, None] * zeta
    d_gate = (d_hidden * upval * sig * (1.0 + gate * (1.0 - sig))).astype(jnp.bfloat16)
    d_up = (d_hidden * act).astype(jnp.bfloat16)
    part_x = lax.dot_general(
        d_gate, w_gate, (((1,), (1,)), ((), ())), preferred_element_type=jnp.float32
    )
    part_x = part_x + lax.dot_general(
        d_up, w_up, (((1,), (1,)), ((), ())), preferred_element_type=jnp.float32
    )
    return part_x.astype(jnp.bfloat16), part_p


def pad_column(values, rows):
    col = jnp.zeros((rows, PAD), jnp.bfloat16)
    return col.at[:, 0].set(values.astype(jnp.bfloat16))


def on_device(tokens, grad_out, expert_ids, route_weight, gate_weight, up_weight, down_weight):
    feats = tokens[0]
    grads = grad_out[0]
    route_ids = expert_ids[0].reshape(-1)
    route_w = route_weight[0].reshape(-1)
    w_gate = lax.all_gather(gate_weight[0, 0], "ex")
    w_up = lax.all_gather(up_weight[0, 0], "ex")
    w_down = lax.all_gather(down_weight[0, 0], "ex")
    groups = lax.axis_size("ez")
    tok_count, width = feats.shape
    rows = tok_count * TOPK
    onehot = (route_ids[:, None] == jnp.arange(groups, dtype=jnp.int32)[None, :]).astype(jnp.int32)
    before = jnp.cumsum(onehot, axis=0) - onehot
    slot = jnp.sum(before * onehot, axis=1)
    place = route_ids * CAP + slot
    table = (place[None, :] == jnp.arange(groups * CAP, dtype=jnp.int32)[:, None]).astype(
        jnp.bfloat16
    )
    packed = jnp.concatenate(
        [jnp.repeat(feats, TOPK, axis=0), jnp.repeat(grads, TOPK, axis=0), pad_column(route_w, rows)],
        axis=1,
    )
    send = jnp.dot(table, packed, preferred_element_type=jnp.float32).astype(jnp.bfloat16)
    recv = lax.all_to_all(
        send.reshape(groups, CAP, -1), "ez", split_axis=0, concat_axis=0, tiled=True
    ).reshape(groups * CAP, -1)
    rows_x = recv[:, :width]
    rows_g = recv[:, width : 2 * width]
    rows_p = recv[:, 2 * width]
    sum_x = None
    sum_p = None
    for q in range(w_gate.shape[0]):
        part_x, part_p = shard_terms(rows_x, rows_g, rows_p, w_gate[q], w_up[q], w_down[q])
        if sum_x is None:
            sum_x = part_x.astype(jnp.float32)
            sum_p = part_p.astype(jnp.float32)
        else:
            sum_x = sum_x + part_x.astype(jnp.float32)
            sum_p = sum_p + part_p.astype(jnp.float32)
    reply = jnp.concatenate(
        [sum_x.astype(jnp.bfloat16), pad_column(sum_p.astype(jnp.bfloat16), groups * CAP)], axis=1
    )
    back = lax.all_to_all(
        reply.reshape(groups, CAP, -1), "ez", split_axis=0, concat_axis=0, tiled=True
    ).reshape(groups * CAP, -1)
    picked = jnp.take(back, place, axis=0)
    input_grad = jnp.sum(
        picked[:, :width].astype(jnp.float32).reshape(tok_count, TOPK, width), axis=1
    ).astype(jnp.bfloat16)
    gate_grad = picked[:, width].reshape(tok_count, TOPK)
    handed = from_behind(input_grad, "section", -1)
    return (handed[None], gate_grad[None])


def solution(mesh):
    sections = mesh.shape["section"]
    experts = mesh.shape["expert"]
    grid = mesh.devices.reshape(sections, experts // SPLIT, SPLIT)
    split_mesh = Mesh(grid, ("section", "ez", "ex"))
    spec3 = P("section", ("ez", "ex"), None)
    spec4 = P("section", ("ez", "ex"), None, None)
    in_specs = (spec3, spec3, spec3, spec3, spec4, spec4, spec4)
    out_specs = (spec3, spec3)
    return jax.shard_map(
        on_device, mesh=split_mesh, in_specs=in_specs, out_specs=out_specs, check_vma=False
    )
```

time: 666 us -> 283 us (0.42)
  waiting for transfers between devices: 553 us -> 202 us
  starting transfers between devices: 57.5 us -> 33.9 us
  blocking collectives: 18.8 us -> 0 us
  between operations: 0.84 us -> 14 us
    all_to_all x4 -> x2, waiting for transfers between devices: 553 us -> 141 us  [the longest x1 94.1 us: on_device(): lax.all_to_all(send.reshape(groups, CAP, -1), 'ez', split_axis=0, concat_...]
    all_gather x0 -> x3, waiting for transfers between devices: none -> 51.6 us  [the longest x1 51.6 us: on_device(): w_down = lax.all_gather(down_weight[0, 0], 'ex')]
    all_to_all x4 -> x2, starting transfers between devices: 49.9 us -> 27.7 us  [the longest x1 15.7 us: on_device(): lax.all_to_all(send.reshape(groups, CAP, -1), 'ez', split_axis=0, concat_...]
    all_to_all x1 -> x0, blocking collectives: 18.8 us -> none  [on_device(): lax.all_to_all(part_p, 'expert', split_axis=0, concat_axis=0, tiled=True)]
    ppermute x1, waiting for transfers between devices: 0.01 us -> 7.34 us  [from_behind(): return lax.ppermute(block, axis, route)]
    dot_general x8 -> x21, matrix products: 19 us -> 21.6 us  [the longest x4 6.73 us: shard_terms(): upval = jnp.dot(rows_x, w_up, preferred_element_type=jnp.float32)]
  transfers between devices with their start and end apart: 5 -> 6, of which waited for: 4 -> 4; matrix products, arithmetic and copies ran while one was open for 2% -> 6% of each run, Pallas kernels for 0% -> 0%
where the time goes in v1:
time: 283 us
  waiting for transfers between devices  202 us (71%)
  starting transfers between devices  33.9 us (12%)
  matrix products  21.6 us (8%)
  between operations  14 us (5%)
  local copies, waits for them, and re-layouts  5.32 us (2%)
  other arithmetic  5.27 us (2%)
    all_to_all x1, waiting for transfers between devices, on_device(): lax.all_to_all(send.reshape(groups, CAP, -1), 'ez', split_axis=0, concat_...  94.1 us
    all_gather x1, waiting for transfers between devices, on_device(): w_down = lax.all_gather(down_weight[0, 0], 'ex')  51.6 us
    all_to_all x1, waiting for transfers between devices, on_device(): lax.all_to_all(reply.reshape(groups, CAP, -1), 'ez', split_axis=0, concat...  47.3 us
    all_to_all x1, starting transfers between devices, on_device(): lax.all_to_all(send.reshape(groups, CAP, -1), 'ez', split_axis=0, concat_...  15.7 us
    all_to_all x1, starting transfers between devices, on_device(): lax.all_to_all(reply.reshape(groups, CAP, -1), 'ez', split_axis=0, concat...  12 us
    ppermute x1, waiting for transfers between devices, from_behind(): return lax.ppermute(block, axis, route)  7.34 us
    dot_general x4, matrix products, shard_terms(): upval = jnp.dot(rows_x, w_up, preferred_element_type=jnp.float32)  6.73 us
    ppermute x1, starting transfers between devices, from_behind(): return lax.ppermute(block, axis, route)  6.07 us
  transfers between devices with their start and end apart: 6, of which 4 were waited for; matrix products, arithmetic and copies ran while one was open for 6% of the time, Pallas kernels for 0%

profile of v1, /device:TPU:1, one launch (start us, length us, event | category | flops | bytes accessed | tf_op | source)
XLA Modules:
  0.0 282.5 jit_solution(13251392504767455158)
XLA Ops:
  7.2 0.0 copy-start.7
  7.2 0.0 copy-start.9
  7.2 0.0 copy-start.10
  7.2 0.0 all-gather.9.cloned.1.call-start
  7.2 0.7 all-gather.9.cloned.1.call-update
  7.9 0.0 all-gather.11.cloned.1.call-start
  8.0 0.7 all-gather.11.cloned.1.call-update
  8.7 0.6 compare_reduce_fusion
  9.3 1.3 fusion.73
  10.6 0.1 copy.17
  10.8 0.7 fusion.68
  11.5 0.2 reduce_window_sum.11
  11.7 0.0 copy-done.7
  11.7 0.2 select_reduce_fusion
  11.9 0.0 copy-done.9
  11.9 0.0 copy-done.10
  11.9 2.1 convolution_convert_fusion
  14.0 15.7 %all-to-all-start = ((bf16[16,16,4224]{2,1,0:T(8,128)(2,1)}), bf16[16,16,4224]{2,1,0:T(8,128)(2,1)S(1)}, u32[]{:S(2)}, u32[]{:S(2)}) async-start(bf16[16,16,4224]{2,1,0:T(8,128)(2,1)} %bitcast.87), calls=%async_computation | async-start | bytes 4325376 | tf_op jit(solution)/shard_map/all_to_all | solution.py:69
  29.7 0.0 all-gather.7.cloned.1.call-start
  29.7 0.7 all-gather.7.cloned.1.call-update
  30.4 94.1 %all-to-all-done = bf16[16,16,4224]{2,1,0:T(8,128)(2,1)S(1)} async-done(((bf16[16,16,4224]{2,1,0:T(8,128)(2,1)}), bf16[16,16,4224]{2,1,0:T(8,128)(2,1)S(1)}, u32[]{:S(2)}, u32[]{:S(2)}) %all-to-all-start) | async-done | bytes 2162720 | tf_op jit(solution)/shard_map/all_to_all | solution.py:69
  124.5 0.1 convert_reduce_fusion
  124.6 0.0 all-gather.9.cloned.1.call-done
  124.7 2.5 fusion.35
  127.1 2.5 fusion.32
  129.6 1.9 fusion.37
  131.5 0.0 copy-start
  131.5 1.9 fusion.34
  133.4 0.0 copy-done.2
  133.4 1.3 fusion.29
  134.7 0.0 copy-done
  134.7 0.5 fusion.31
  135.2 0.5 fusion.26
  135.8 0.5 fusion.28
  136.3 51.6 %all-gather.7.cloned.1.call-done = bf16[4,1,256,2048]{3,2,1,0:T(8,128)(2,1)} async-done(((bf16[1,1,256,2048]{3,2,1,0:T(8,128)(2,1)}), bf16[4,1,256,2048]{3,2,1,0:T(8,128)(2,1)}) %all-gather.7.cloned.1.call-update) | async-done | bytes 4194320 | tf_op jit(solution)/shard_map/all_gather | solution.py:53
  187.9 1.9 multiply_reduce_fusion
  189.8 0.0 copy-done.5
  189.8 0.8 copy-done.8
  190.6 0.5 multiply_reduce_fusion.1
  191.1 0.5 copy-done.4
  191.6 0.5 multiply_reduce_fusion.2
  192.1 0.0 copy-start.1
  192.1 0.5 multiply_reduce_fusion.3
  192.6 0.9 broadcast_select_fusion.1
  193.5 0.1 reshape.224
  193.6 0.7 copy-done.1
  194.3 0.6 fusion.36
  194.8 0.7 copy-done.3
  195.6 0.5 fusion.11
  196.1 0.6 fusion.33
  196.6 0.5 fusion.9
  197.2 0.6 fusion.30
  197.7 0.5 fusion.7
  198.3 0.6 fusion.27
  198.8 0.7 fusion.5
  199.5 1.1 fusion.14
  200.6 12.0 %all-to-all-start.1 = ((bf16[16,16,2176]{2,1,0:T(8,128)(2,1)}), bf16[16,16,2176]{2,1,0:T(8,128)(2,1)S(1)}, u32[]{:S(2)}, u32[]{:S(2)}) async-start(bf16[16,16,2176]{2,1,0:T(8,128)(2,1)} %bitcast.18), calls=%async_computation.1 | async-start | bytes 2228224 | tf_op jit(solution)/shard_map/all_to_all | solution.py:88
  212.7 47.3 %all-to-all-done.1 = bf16[16,16,2176]{2,1,0:T(8,128)(2,1)S(1)} async-done(((bf16[16,16,2176]{2,1,0:T(8,128)(2,1)}), bf16[16,16,2176]{2,1,0:T(8,128)(2,1)S(1)}, u32[]{:S(2)}, u32[]{:S(2)}) %all-to-all-start.1) | async-done | bytes 1114144 | tf_op jit(solution)/shard_map/all_to_all | solution.py:88
  260.0 1.0 gather_fusion
  261.0 0.1 broadcast_select_fusion
  261.2 6.1 %collective-permute-start = (bf16[128,2048]{1,0:T(8,128)(2,1)S(1)}, bf16[128,2048]{1,0:T(8,128)(2,1)S(1)}, u32[]{:S(2)}, u32[]{:S(2)}) collective-permute-start(bf16[128,2048]{1,0:T(8,128)(2,1)S(1)} %slice.125), channel_id=1, source_target_pairs={{64,0},{128,64},{192,128},{256,192},{320,256},{384,320},{448,384},... | collective-permute-start | bytes 1572872 | tf_op jit(solution)/shard_map/ppermute | solution.py:16
  267.2 0.6 slice_reduce_fusion
  267.9 7.3 %collective-permute-done = bf16[128,2048]{1,0:T(8,128)(2,1)S(1)} collective-permute-done((bf16[128,2048]{1,0:T(8,128)(2,1)S(1)}, bf16[128,2048]{1,0:T(8,128)(2,1)S(1)}, u32[]{:S(2)}, u32[]{:S(2)}) %collective-permute-start) | collective-permute-done | bytes 524320 | tf_op jit(solution)/shard_map/ppermute | solution.py:16
  275.2 0.8 copy.19
  (12 shorter events, 0.1 us)
Async XLA Ops:
  7.2 4.5 %copy-start.7 = (s32[1,128,1]{1,2,0:T(1,128)S(1)}, s32[1,128,1]{1,2,0:T(1,128)}, u32[]{:S(2)}) copy-start(s32[1,128,1]{1,2,0:T(1,128)} %param.13) | copy-start | bytes 1540
  7.2 4.7 %copy-start.9 = (bf16[1,128,2048]{2,1,0:T(8,128)(2,1)S(1)}, bf16[1,128,2048]{2,1,0:T(8,128)(2,1)}, u32[]{:S(2)}) copy-start(bf16[1,128,2048]{2,1,0:T(8,128)(2,1)} %param.12) | copy-start | bytes 1572868
  7.2 4.7 %copy-start.10 = (bf16[1,128,2048]{2,1,0:T(8,128)(2,1)S(1)}, bf16[1,128,2048]{2,1,0:T(8,128)(2,1)}, u32[]{:S(2)}) copy-start(bf16[1,128,2048]{2,1,0:T(8,128)(2,1)} %param.11) | copy-start | bytes 1572868
  7.2 117.5 %all-gather.9.cloned.1.call-start = ((), (), s32[]{:S(2)}) async-start(), calls=%async_computation.3 | async-start | bytes 5242880 | tf_op jit(solution)/shard_map/all_gather | solution.py:52
  7.9 121.7 %all-gather.11.cloned.1.call-start = ((), (), s32[]{:S(2)}) async-start(), calls=%async_computation.4 | async-start | bytes 5242880 | tf_op jit(solution)/shard_map/all_gather | solution.py:51
  14.0 110.6 %all-to-all-start = ((bf16[16,16,4224]{2,1,0:T(8,128)(2,1)}), bf16[16,16,4224]{2,1,0:T(8,128)(2,1)S(1)}, u32[]{:S(2)}, u32[]{:S(2)}) async-start(bf16[16,16,4224]{2,1,0:T(8,128)(2,1)} %bitcast.87), calls=%async_computation | async-start | bytes 4325376 | tf_op jit(solution)/shard_map/all_to_all | solution.py:69
  29.7 158.2 %all-gather.7.cloned.1.call-start = ((), (), s32[]{:S(2)}) async-start(), calls=%async_computation.2 | async-start | bytes 5242880 | tf_op jit(solution)/shard_map/all_gather | solution.py:53
  129.6 3.8 %copy-start.2 = (bf16[4,1,2048,256]{3,2,1,0:T(8,128)(2,1)S(1)}, bf16[4,1,2048,256]{3,2,1,0:T(8,128)(2,1)}, u32[]{:S(2)}) copy-start(bf16[4,1,2048,256]{3,2,1,0:T(8,128)(2,1)} %all-gather.9.cloned.1.call-done) | copy-start | bytes 12582916
  131.5 3.2 %copy-start = (bf16[4,1,2048,256]{3,2,1,0:T(8,128)(2,1)S(1)}, bf16[4,1,2048,256]{3,2,1,0:T(8,128)(2,1)}, u32[]{:S(2)}) copy-start(bf16[4,1,2048,256]{3,2,1,0:T(8,128)(2,1)} %all-gather.11.cloned.1.call-done) | copy-start | bytes 12582916
  187.9 1.9 copy-start.5
  187.9 2.7 copy-start.8
  190.6 0.9 copy-start.4
  191.6 2.0 copy-start.6
  192.1 2.2 copy-start.1
  192.1 3.5 %copy-start.3 = (bf16[4,1,2048,256]{3,2,1,0:T(8,128)(2,1)S(1)}, bf16[4,1,2048,256]{3,2,1,0:T(8,128)(2,1)}, u32[]{:S(2)}) copy-start(bf16[4,1,2048,256]{3,2,1,0:T(8,128)(2,1)} %all-gather.9.cloned.1.call-done) | copy-start | bytes 12582916
  200.6 59.4 %all-to-all-start.1 = ((bf16[16,16,2176]{2,1,0:T(8,128)(2,1)}), bf16[16,16,2176]{2,1,0:T(8,128)(2,1)S(1)}, u32[]{:S(2)}, u32[]{:S(2)}) async-start(bf16[16,16,2176]{2,1,0:T(8,128)(2,1)} %bitcast.18), calls=%async_computation.1 | async-start | bytes 2228224 | tf_op jit(solution)/shard_map/all_to_all | solution.py:88
  261.2 14.0 %collective-permute-start = (bf16[128,2048]{1,0:T(8,128)(2,1)S(1)}, bf16[128,2048]{1,0:T(8,128)(2,1)S(1)}, u32[]{:S(2)}, u32[]{:S(2)}) collective-permute-start(bf16[128,2048]{1,0:T(8,128)(2,1)S(1)} %slice.125), channel_id=1, source_target_pairs={{64,0},{128,64},{192,128},{256,192},{320,256},{384,320},{448,384},... | collective-permute-start | bytes 1572872 | tf_op jit(solution)/shard_map/ppermute | solution.py:16
Sparse Core Ops, SparseCore 0:
  10.1 60.9 all-gather.8
  73.2 56.2 all-gather.10
  131.6 56.2 all-gather.6
